TPU v7x, 32 devices: a whole 2x2x4 slice. The times are simulated.
32 devices in a mesh: gx: 8 (over z, y), gy: 4 (over x, core).
Axes of the slice: x: 2, y: 2, z: 4, core: 2. Of those that a mesh axis runs over, the one named last changes fastest.
Arguments:
- queries: bfloat16 [8, 768, 2560], P('gx', 'gy'), may hold values from -7 to 7
- new_kv: bfloat16 [8, 768, 512], P('gx', 'gy'), may hold values from -7 to 7
- cache_pool: bfloat16 [8, 2048, 512], P('gx', 'gy'), may hold values from -6 to 6
- lengths: int32 [8], P('gx'), may hold values from 0 to 32768, as said below
- owner: int32 [8, 4], P('gx'), may hold values from 0 to 3, each once within a row
- w_out: bfloat16 [2560, 2560], P(None, ('gx', 'gy')), may hold values from -0.125 to 0.125
- last_residual: bfloat16 [8, 2560], P(None, ('gx', 'gy')), may hold values from -6 to 6
- norm_gain: bfloat16 [2560], replicated, may hold values from 0.5 to 1.5
- head: bfloat16 [256000, 2560], P(('gx', 'gy')), may hold values from -11 to 11
- targets: int32 [8], replicated, may hold values from 0 to 255999
Outputs:
- mixed_out: bfloat16 [8, 768, 2560], P('gx', 'gy')
- new_cache: bfloat16 [8, 2048, 512], P('gx', 'gy')
- log_norm: float32 [8], replicated
- top_logit: float32 [8], replicated
- target_logprob: float32 [8], replicated
Inputs may be any that keep to these rules, and one draw needn't show every extreme that they name: `lengths`: in every draw one request has seen 32768 tokens and one has seen none. `owner`: each row names every block index once.
All inputs are finite; a program needn't handle non-finite values.
Results may differ from a plain program's by a relative error of at most 0.0042.
Values may be sent and summed in bfloat16 or wider, within the bound.
No kernel may reach another device: no remote copies, remote signals or barrier semaphores. Data moves between devices by JAX's collectives and lax.ppermute only.
A program may use at most 128 MiB of HBM per device.

v0:
```python
import math
import jax
import jax.numpy as jnp
from jax import lax
from jax.sharding import PartitionSpec as P


def on_device(
    queries, new_kv, cache_pool, lengths, owner, w_out, last_residual, norm_gain, head, targets
):
    req_local, new_local, model_cols = queries.shape
    slot_count = cache_pool.shape[1]
    entry_width = new_kv.shape[2]
    head_dim = entry_width // 2
    head_count = model_cols // head_dim
    group_pos = lax.axis_size("gy")
    my_index = lax.axis_index("gy")
    new_total = new_local * group_pos
    window_len = slot_count * group_pos
    keep_len = window_len - new_total
    score_scale = 1.0 / math.sqrt(head_dim)
    query_heads = queries.reshape(req_local, new_local, head_count, head_dim)
    query_pos = my_index * new_local + jnp.arange(new_local, dtype=jnp.int32)
    first_slot = window_len - lengths
    block_ids = jnp.arange(group_pos, dtype=jnp.int32)
    matches = owner[:, :, None] == block_ids[None, None, :]
    logical = jnp.sum(jnp.where(matches, block_ids[None, :, None], 0), axis=1)
    own_block = lax.dynamic_index_in_dim(logical, my_index, axis=1, keepdims=False)
    slot_ids = jnp.arange(slot_count, dtype=jnp.int32)
    new_ids = jnp.arange(new_local, dtype=jnp.int32)
    target_slot = own_block[:, None] * slot_count + slot_ids[None, :]
    from_old = target_slot < keep_len
    old_slot = jnp.minimum(target_slot + new_total, window_len - 1)
    old_block = jnp.take_along_axis(owner, old_slot // slot_count, axis=1)
    pool_row = old_block * slot_count + old_slot % slot_count
    new_row = jnp.maximum(target_slot - keep_len, 0)
    source_cache = jnp.where(from_old, pool_row, -1)
    source_new = jnp.where(from_old, -1, new_row)

    def cache_keys(shard_ids):
        chosen = jnp.take(logical, shard_ids, axis=1)
        slot_pos = (chosen[:, :, None] * slot_count + slot_ids[None, None, :]).reshape(
            req_local, -1
        )
        return (slot_pos[:, None, :] >= query_pos[None, :, None]) & (
            slot_pos[:, None, :] >= first_slot[:, None, None]
        )

    def new_keys(shard_ids):
        positions = (shard_ids[:, None] * new_local + new_ids[None, :]).reshape(-1)
        seen_new = positions[None, :] <= query_pos[:, None]
        return seen_new[None]

    def attend(carried, key_rows, visible):
        running_max, weight_sum, accumulated = carried
        scores = (
            jnp.einsum(
                "rthd,rnd->rthn",
                query_heads,
                key_rows[:, :, :head_dim],
                preferred_element_type=jnp.float32,
            )
            * score_scale
        )
        allowed = visible[:, :, None, :]
        block_max = jnp.max(jnp.where(allowed, scores, -1e30), axis=3)
        new_max = jnp.maximum(running_max, block_max)
        weights = jnp.where(allowed, jnp.exp(scores - new_max[..., None]), 0.0)
        rescale = jnp.exp(running_max - new_max)
        weight_sum = rescale * weight_sum + jnp.sum(weights, axis=3)
        accumulated = rescale[..., None] * accumulated + jnp.einsum(
            "rthn,rnd->rthd",
            weights.astype(jnp.bfloat16),
            key_rows[:, :, head_dim:],
            preferred_element_type=jnp.float32,
        )
        return (new_max, weight_sum, accumulated)

    def copy_rows(fresh_block, part_rows, source, base_row):
        local_row = source - base_row
        inside = (local_row >= 0) & (local_row < part_rows.shape[1])
        clipped = jnp.clip(local_row, 0, part_rows.shape[1] - 1)
        picked = jnp.take_along_axis(part_rows, clipped[:, :, None], axis=1)
        return jnp.where(inside[:, :, None], picked, fresh_block)

    def make_step(shard_width, source, layout_kind, carried, shard_rows):
        shard_count = shard_rows.shape[1] // shard_width
        group_size = math.gcd(shard_count, 4)

        def turn_body(turn_index, inner_state):
            offset = turn_index * group_size * shard_width
            part_rows = lax.dynamic_slice_in_dim(shard_rows, offset, group_size * shard_width, 1)
            shard_ids = turn_index * group_size + jnp.arange(group_size, dtype=jnp.int32)
            if layout_kind == "cache":
                key_rows = part_rows
                visible = cache_keys(shard_ids)
            else:
                key_rows = part_rows
                visible = new_keys(shard_ids)
            softmax_state = lax.cond(
                jnp.any(visible),
                lambda state: attend(state, key_rows, visible),
                lambda state: state,
                inner_state[:3],
            )
            fresh_block = copy_rows(inner_state[3], part_rows, source, offset)
            return softmax_state + (fresh_block,)

        return lax.fori_loop(0, shard_count // group_size, turn_body, carried)

    initial = (
        jnp.full((req_local, new_local, head_count), -1e30, jnp.float32),
        jnp.zeros((req_local, new_local, head_count), jnp.float32),
        jnp.zeros((req_local, new_local, head_count, head_dim), jnp.float32),
        jnp.zeros((req_local, slot_count, entry_width), jnp.bfloat16),
    )
    carried = make_step(
        slot_count,
        source_cache,
        "cache",
        initial,
        lax.all_gather(cache_pool, "gy", axis=1, tiled=True),
    )
    carried = make_step(
        new_local, source_new, "new", carried, lax.all_gather(new_kv, "gy", axis=1, tiled=True)
    )
    running_max, weight_sum, accumulated, fresh_block = carried
    mixed_out = (
        (accumulated / weight_sum[..., None])
        .astype(jnp.bfloat16)
        .reshape(req_local, new_local, model_cols)
    )
    last_local = mixed_out[:, new_local - 1, :]
    group_req = lax.axis_size("gx")
    holder = (my_index == group_pos - 1).astype(jnp.float32)
    padded = jnp.zeros((req_local * group_req, model_cols), jnp.float32)
    padded = lax.dynamic_update_slice_in_dim(
        padded, last_local.astype(jnp.float32) * holder, lax.axis_index("gx") * req_local, 0
    )
    last_mixed = lax.psum(padded, ("gx", "gy")).astype(jnp.bfloat16)
    last_hidden = (
        last_residual.astype(jnp.float32)
        + jnp.dot(last_mixed, w_out, preferred_element_type=jnp.float32)
    ).astype(jnp.bfloat16)
    full_hidden = lax.all_gather(last_hidden, ("gx", "gy"), axis=1, tiled=True).astype(jnp.float32)
    normed = (
        full_hidden
        * lax.rsqrt(jnp.mean(full_hidden * full_hidden, axis=1, keepdims=True) + 1e-06)
        * norm_gain.astype(jnp.float32)
    ).astype(jnp.bfloat16)
    logits = lax.dot_general(
        normed, head, (((1,), (1,)), ((), ())), preferred_element_type=jnp.float32
    )
    vocab_local = head.shape[0]
    local_target = targets - lax.axis_index(("gx", "gy")) * vocab_local
    target_hit = jnp.arange(vocab_local, dtype=jnp.int32)[None, :] == local_target[:, None]
    picked = jnp.sum(jnp.where(target_hit, logits, 0.0), axis=1)
    local_top = jnp.max(logits, axis=1)
    top_logit = lax.pmax(local_top, ("gx", "gy"))
    exp_total, picked = lax.psum(
        (jnp.sum(jnp.exp(logits - top_logit[:, None]), axis=1), picked), ("gx", "gy")
    )
    log_norm = top_logit + jnp.log(exp_total)
    return (mixed_out, fresh_block, log_norm, top_logit, picked - log_norm)


def solution(mesh):
    placed = (
        P("gx", "gy", None),
        P("gx", "gy", None),
        P("gx", "gy", None),
        P("gx"),
        P("gx", None),
        P(None, ("gx", "gy")),
        P(None, ("gx", "gy")),
        P(),
        P(("gx", "gy"), None),
        P(),
    )
    return jax.shard_map(
        on_device,
        mesh=mesh,
        in_specs=placed,
        out_specs=(P("gx", "gy", None), P("gx", "gy", None), P(), P(), P()),
        check_vma=False,
    )
```

profile of v0, /device:TPU:0, one launch (start us, length us, event | category | flops | bytes accessed | tf_op | source)
XLA Modules:
  0.0 262.6 jit_solution(15581894182387955175)
XLA Ops:
  7.2 0.0 all-gather.3.cloned.1.call-start
  7.2 0.7 all-gather.3.cloned.1.call-update
  8.6 1.5 copy.34
  10.2 0.7 select_reduce_fusion.3
  10.9 0.6 gather_fusion
  11.6 0.1 add.795
  11.6 1.1 compare_and_fusion
  13.4 0.1 iota_add_fusion
  13.5 0.1 add.792
  13.6 0.8 compare_reduce_fusion
  15.0 0.7 convert_element_type.62
  15.7 0.6 dynamic-slice.3
  17.0 1.5 fusion.55
  18.4 2.6 compare_select_fusion
  21.1 14.6 %all_gather.10 = bf16[1,768,512]{2,1,0:T(8,128)(2,1)S(1)} all-gather(bf16[1,192,512]{2,1,0:T(8,128)(2,1)} %param.15), channel_id=1, replica_groups=mesh['gx'=8,'gy'=4] {'gy'}, dimensions={1}, use_global_device_ids=true | all-gather | bytes 983040 | tf_op jit(solution)/shard_map/all_gather | solution.py:125
  35.7 2.6 gather_fusion.1
  38.3 1.4 broadcast_in_dim.173
  39.7 0.6 compare_and_fusion.3
  40.3 2.6 compare_select_fusion.3
  42.9 0.6 pad_clamp_fusion
  43.5 0.6 compare_and_fusion.2
  44.1 0.6 compare_and_fusion.1
  44.7 15.8 %conditional.2 = ((f32[1,192,10]{1,2,0:T(8,128)S(1)}, f32[1,192,10]{1,2,0:T(8,128)S(1)}, f32[1,192,10,256]{3,1,2,0:T(8,128)})) conditional(s32[]{:T(128)} %convert_element_type.54, (f32[1,192,10]{1,2,0:T(8,128)S(1)}, f32[1,192,10]{1,2,0:T(8,128)S(1)}, f32[1,192,10,256]{3,1,2,0:T(8,128)}) %tuple.31, (pred[1,192,2048]{2,1,0:T(8,128)(4,1)S(1)}, ...), branch_computations={%region_3.4_spmd, %region_4.7_spmd} | conditional | flops 4070774272 | bytes 63906876 | solution.py:100
  44.7 5.7 %select_reduce_fusion = (f32[192,10]{0,1:T(8,128)S(1)}, f32[192,10,2048]{2,0,1:T(8,128)S(1)}) fusion(pred[192,2048]{1,0:T(8,128)(4,1)S(1)} %bitcast.103, bf16[1,2048,512]{2,1,0:T(8,128)(2,1)} %get-tuple-element.118, bf16[1,192,10,256]{1,3,2,0:T(8,128)(2,1)S(1)} %get-tuple-element.209), kind=kOutput, calls=%fused_computation.4 | convolution fusion | flops 2025060480 | bytes 18161152 | tf_op jit(solution)/shard_map/while/body/eval_jaxpr/cond/branch_1_fun/rthd,rnd->rthn/dot_general | solution.py:57
  50.4 5.4 %bitcast_add_fusion = f32[1,192,10,256]{3,1,2,0:T(8,128)} fusion(f32[1,192,10,256]{3,1,2,0:T(8,128)} %get-tuple-element.120, f32[192,10,2048]{2,0,1:T(8,128)S(1)} %get-tuple-element.243, f32[192,10]{0,1:T(8,128)S(1)} %bitcast.109, pred[192,2048]{1,0:T(8,128)(4,1)S(1)} %bitcast.104, bf16[1,2048,512]{2,1,0:T(8,128)(2,1)S(1)} %copy-done.2, ...), kind=kOutput, calls=%fused_computation.9 | convolution fusion | flops 2029977600 | bytes 21135360 | tf_op jit(solution)/shard_map/while/body/eval_jaxpr/cond/branch_1_fun/rthn,rnd->rthd/dot_general | solution.py:71
  55.8 4.7 %fusion.1 = f32[192,10]{0,1:T(8,128)S(1)} fusion(f32[192,10,2048]{2,0,1:T(8,128)S(1)} %get-tuple-element.243, f32[192,10]{0,1:T(8,128)S(1)} %bitcast.110, pred[192,2048]{1,0:T(8,128)(4,1)S(1)} %bitcast.105), kind=kLoop, calls=%fused_computation.6 | loop fusion | flops 15726720 | bytes 16137216 | tf_op jit(solution)/shard_map/while/body/eval_jaxpr/cond/branch_1_fun/reduce_sum | solution.py:70
  60.5 7.6 %conditional.3 = ((f32[1,192,10]{1,2,0:T(8,128)S(1)}, f32[1,192,10,256]{3,1,2,0:T(8,128)})) conditional(s32[]{:T(128)} %convert_element_type.53, (f32[1,192,10]{1,2,0:T(8,128)S(1)}, f32[1,192,10,256]{3,1,2,0:T(8,128)}) %tuple.33, (s32[768]{0:T(1024)S(1)}, s32[192]{0:T(256)S(1)}, bf16[1,192,10,256]{1,3,2,0:T(8,128)(2,1)S(1)}, ...), branch_computations={%region_7.8_spmd, %region_8.11_spmd} | conditional | flops 1527307776 | bytes 24442648 | solution.py:100
  60.5 0.1 broadcast_compare_fusion
  60.6 1.7 select_reduce_fusion.1
  62.4 3.7 %bitcast_add_fusion.2 = f32[1,192,10,256]{3,1,2,0:T(8,128)} fusion(f32[1,192,10,256]{3,1,2,0:T(8,128)} %get-tuple-element.138, f32[192,10,768]{2,0,1:T(8,128)S(1)} %get-tuple-element.241, f32[192,10]{0,1:T(8,128)S(1)} %get-tuple-element.239, pred[192,768]{1,0:T(8,128)(4,1)S(1)} %broadcast_compare_fusion, f32[192,10]{0,1:T(8,128)S(1)} %get-tuple-element.238, ...), kind=kOutput, calls=%fused_computation.31 | convolution fusion | flops 761856000 | bytes 10403840 | tf_op jit(solution)/shard_map/while/body/eval_jaxpr/cond/branch_1_fun/rthn,rnd->rthd/dot_general | solution.py:71
  66.1 1.7 fusion.17
  68.1 1.9 divide_convert_fusion
  70.0 0.6 copy.37
  70.6 1.4 copy.39
  71.9 0.6 multiply_reduce_fusion
  72.6 0.3 dynamic_update_slice.3
  72.8 41.4 %psum.21 = bf16[8,2560]{1,0:T(8,128)(2,1)S(1)} all-reduce(f32[8,2560]{1,0:T(8,128)S(1)} %dynamic_update_slice.3), channel_id=1, replica_groups=mesh['gx'=8,'gy'=4] {'gx','gy'}, use_global_device_ids=true, to_apply=%region_11.12 | all-reduce | flops 20480 | bytes 122880 | tf_op jit(solution)/shard_map/psum | solution.py:140
  114.3 0.2 fusion.37
  114.5 40.6 %all-gather = bf16[32,80,8]{1,2,0:T(8,128)(2,1)S(1)} all-gather(bf16[1,80,8]{1,2,0:T(8,128)(2,1)S(1)} %fusion.37), channel_id=1, replica_groups=mesh['gx'=8,'gy'=4] {'gx','gy'}, dimensions={0}, use_global_device_ids=true | all-gather | bytes 42240 | tf_op jit(solution)/shard_map/all_gather | solution.py:145
  155.1 0.1 reshape.940
  155.2 0.1 multiply_reduce_fusion.1
  155.4 17.4 %fusion.56 = (f32[8]{0:T(128)S(1)}, f32[8,8000]{1,0:T(8,128)S(1)}) fusion(bf16[8000,2560]{1,0:T(8,128)(2,1)} %param.22, f32[2560,8]{0,1:T(8,128)S(1)} %reshape.940, f32[2560]{0:T(1024)S(1)} %convert_element_type.62, f32[8]{0:T(128)S(1)} %add_rsqrt_fusion), kind=kOutput, calls=%fused_computation.123 | convolution fusion | flops 327805440 | bytes 41308224 | tf_op jit(solution)/shard_map/dot_general | solution.py:151
  172.7 36.9 %pmax.7 = f32[8]{0:T(128)S(1)} all-reduce(f32[8]{0:T(128)S(1)} %get-tuple-element.250), channel_id=1, replica_groups=mesh['gx'=8,'gy'=4] {'gx','gy'}, use_global_device_ids=true, to_apply=%region_14.15 | all-reduce | flops 8 | bytes 64 | tf_op jit(solution)/shard_map/pmax | solution.py:159
  209.7 0.3 select_reduce_fusion.2
  209.9 41.2 %all-reduce = (f32[8]{0:T(128)S(1)}, f32[8]{0:T(128)S(1)}) all-reduce(f32[8]{0:T(128)S(1)} %get-tuple-element.227, f32[8]{0:T(128)S(1)} %get-tuple-element.226), channel_id=1, replica_groups=mesh['gx'=8,'gy'=4] {'gx','gy'}, use_global_device_ids=true, to_apply=%region_16.17 | all-reduce | flops 16 | bytes 128 | tf_op jit(solution)/shard_map/psum | solution.py:160
  251.2 0.5 fusion.53
  251.7 2.1 gather_fusion.2
  253.8 1.9 fusion.39
  (36 shorter events, 0.2 us)
Async XLA Ops:
  7.2 107.1 %copy-start = (bf16[2560,80]{0,1:T(8,128)(2,1)S(1)}, bf16[2560,80]{0,1:T(8,128)(2,1)}, u32[]{:S(2)}) copy-start(bf16[2560,80]{0,1:T(8,128)(2,1)} %param.19) | copy-start | bytes 1228804
  7.2 36.3 %copy-start.6 = (s32[8]{0:T(128)S(1)}, s32[8]{0:T(128)}, u32[]{:S(2)}) copy-start(s32[8]{0:T(128)} %param.23) | copy-start | bytes 100
  7.2 37.5 %all-gather.3.cloned.1.call-start = ((), (), s32[]{:S(2)}) async-start(), calls=%async_computation | async-start | bytes 2621440 | tf_op jit(solution)/shard_map/all_gather | solution.py:122
  44.7 5.7 %copy-start.2 = (bf16[1,2048,512]{2,1,0:T(8,128)(2,1)S(1)}, bf16[1,2048,512]{2,1,0:T(8,128)(2,1)}, u32[]{:S(2)}) copy-start(bf16[1,2048,512]{2,1,0:T(8,128)(2,1)} %get-tuple-element.118) | copy-start | bytes 6291460 | tf_op jit(solution)/shard_map/while/body/eval_jaxpr/cond
  68.1 46.2 %copy-start.4 = (bf16[8,80]{1,0:T(8,128)(2,1)S(1)}, bf16[8,80]{1,0:T(8,128)(2,1)}, u32[]{:S(2)}) copy-start(bf16[8,80]{1,0:T(8,128)(2,1)} %param.20) | copy-start | bytes 3844
  155.3 96.3 %copy-start.1 = (bf16[1,2048,512]{2,1,0:T(8,128)(2,1)S(1)}, bf16[1,2048,512]{2,1,0:T(8,128)(2,1)}, u32[]{:S(2)}) copy-start(bf16[1,2048,512]{2,1,0:T(8,128)(2,1)} %all-gather.3.cloned.1.call-done) | copy-start | bytes 6291460
  155.3 98.4 %copy-start.3 = (bf16[512,512]{1,0:T(8,128)(2,1)S(1)}, bf16[512,512]{1,0:T(8,128)(2,1)}, u32[]{:S(2)}) copy-start(bf16[512,512]{1,0:T(8,128)(2,1)} %gather_fusion.1) | copy-start | bytes 1572868
  209.7 42.0 %copy-start.5 = (f32[8]{0:T(128)}, f32[8]{0:T(128)S(1)}, u32[]{:S(2)}) copy-start(f32[8]{0:T(128)S(1)} %pmax.7) | copy-start | bytes 100
Sparse Core Ops, SparseCore 0:
  9.6 29.4 all-gather.2
where the time goes:
time: 263 us
  blocking collectives  175 us (67%)
  matrix products  34.1 us (13%)
  other arithmetic  23 us (9%)
  between operations  16.9 us (6%)
  local copies, waits for them, and re-layouts  12.9 us (5%)
    psum x1, blocking collectives, on_device(): last_mixed = lax.psum(padded, ('gx', 'gy')).astype(jnp.bfloat16)  41.4 us
    psum x1, blocking collectives, on_device(): lax.psum((jnp.sum(jnp.exp(logits - top_logit[:, None]), axis=1), picked),...  41.2 us
    all_gather x1, blocking collectives, on_device(): lax.all_gather(last_hidden, ('gx', 'gy'), axis=1, tiled=True)  40.6 us
    pmax x1, blocking collectives, on_device(): top_logit = lax.pmax(local_top, ('gx', 'gy'))  36.9 us
    dot_general x1, matrix products, on_device(): lax.dot_general(normed, head, (((1,), (1,)), ((), ())), preferred_element...  17.4 us
    all_gather x1, blocking collectives, on_device(): lax.all_gather(new_kv, 'gy', axis=1, tiled=True)  14.6 us
    dot_general x2, matrix products, attend(): jnp.einsum('rthn,rnd->rthd', weights.astype(jnp.bfloat16), key_rows[:, :,...  9.09 us
    dot_general x2, matrix products, attend(): jnp.einsum('rthd,rnd->rthn', query_heads, key_rows[:, :, :head_dim], pref...  7.42 us
  transfers between devices with their start and end apart: 1, of which 0 were waited for; matrix products, arithmetic and copies ran while one was open for 7% of the time, Pallas kernels for 0%

commit v1 on v0

--- a/solution.py
+++ b/solution.py
@@ -137,7 +137,7 @@
     padded = lax.dynamic_update_slice_in_dim(
         padded, last_local.astype(jnp.float32) * holder, lax.axis_index("gx") * req_local, 0
     )
-    last_mixed = lax.psum(padded, ("gx", "gy")).astype(jnp.bfloat16)
+    last_mixed = lax.psum(lax.psum(padded, "gy"), "gx").astype(jnp.bfloat16)
     last_hidden = (
         last_residual.astype(jnp.float32)
         + jnp.dot(last_mixed, w_out, preferred_element_type=jnp.float32)

time: 263 us -> 288 us (1.095)
  waiting for transfers between devices: 0.68 us -> 24.7 us
  blocking collectives: 175 us -> 170 us
    psum x0 -> x1, waiting for transfers between devices: none -> 24 us  [on_device(): last_mixed = lax.psum(lax.psum(padded, 'gy'), 'gx').astype(jnp.bfloat16)]
    psum x1, blocking collectives: 41.4 us -> 38.5 us  [on_device(): last_mixed = lax.psum(lax.psum(padded, 'gy'), 'gx').astype(jnp.bfloat16)]
  transfers between devices with their start and end apart: 1 -> 2, of which waited for: 0 -> 1; matrix products, arithmetic and copies ran while one was open for 7% -> 9% of each run, Pallas kernels for 0% -> 0%
where the time goes in v1:
time: 288 us; the launch traced here: 287 us
  blocking collectives  170 us (59%)
  matrix products  34.6 us (12%)
  other arithmetic  25.4 us (9%)
  waiting for transfers between devices  24.7 us (9%)
  between operations  16.9 us (6%)
  local copies, waits for them, and re-layouts  15.4 us (5%)
    psum x1, blocking collectives, on_device(): lax.psum((jnp.sum(jnp.exp(logits - top_logit[:, None]), axis=1), picked),...  41.2 us
    all_gather x1, blocking collectives, on_device(): lax.all_gather(last_hidden, ('gx', 'gy'), axis=1, tiled=True)  38.6 us
    psum x1, blocking collectives, on_device(): last_mixed = lax.psum(lax.psum(padded, 'gy'), 'gx').astype(jnp.bfloat16)  38.5 us
    pmax x1, blocking collectives, on_device(): top_logit = lax.pmax(local_top, ('gx', 'gy'))  36.9 us
    psum x1, waiting for transfers between devices, on_device(): last_mixed = lax.psum(lax.psum(padded, 'gy'), 'gx').astype(jnp.bfloat16)  24 us
    dot_general x1, matrix products, on_device(): lax.dot_general(normed, head, (((1,), (1,)), ((), ())), preferred_element...  17.2 us
    all_gather x1, blocking collectives, on_device(): lax.all_gather(new_kv, 'gy', axis=1, tiled=True)  14.6 us
    dot_general x2, matrix products, attend(): jnp.einsum('rthn,rnd->rthd', weights.astype(jnp.bfloat16), key_rows[:, :,...  9.09 us
  transfers between devices with their start and end apart: 2, of which 1 were waited for; matrix products, arithmetic and copies ran while one was open for 9% of the time, Pallas kernels for 0%

profile of v1, /device:TPU:0, one launch (start us, length us, event | category | flops | bytes accessed | tf_op | source)
XLA Modules:
  0.0 287.1 jit_solution(16543143940706282680)
XLA Ops:
  7.2 0.7 all-gather.3.cloned.1.call-update
  8.6 1.5 copy.34
  10.2 0.7 select_reduce_fusion.3
  11.0 0.6 gather_fusion
  11.7 1.1 compare_and_fusion
  13.5 0.1 add.794
  13.6 0.8 compare_reduce_fusion
  15.1 1.3 convert_element_type.62
  16.4 0.6 dynamic-slice.3
  17.6 1.4 fusion.55
  19.0 2.6 compare_select_fusion
  21.7 14.6 %all_gather.10 = bf16[1,768,512]{2,1,0:T(8,128)(2,1)S(1)} all-gather(bf16[1,192,512]{2,1,0:T(8,128)(2,1)} %param.15), channel_id=1, replica_groups=mesh['gx'=8,'gy'=4] {'gy'}, dimensions={1}, use_global_device_ids=true | all-gather | bytes 983040 | tf_op jit(solution)/shard_map/all_gather | solution.py:125
  36.3 2.6 gather_fusion.1
  38.9 1.4 broadcast_in_dim.173
  40.4 0.6 compare_and_fusion.3
  41.0 2.6 compare_select_fusion.3
  43.6 0.6 pad_clamp_fusion
  44.2 0.5 broadcast_subtract_fusion
  44.7 0.6 compare_and_fusion.2
  45.3 0.5 compare_and_fusion.1
  45.8 15.8 %conditional.2 = ((f32[1,192,10]{1,2,0:T(8,128)S(1)}, f32[1,192,10]{1,2,0:T(8,128)S(1)}, f32[1,192,10,256]{3,1,2,0:T(8,128)})) conditional(s32[]{:T(128)} %convert_element_type.54, (f32[1,192,10]{1,2,0:T(8,128)S(1)}, f32[1,192,10]{1,2,0:T(8,128)S(1)}, f32[1,192,10,256]{3,1,2,0:T(8,128)}) %tuple.31, (pred[1,192,2048]{2,1,0:T(8,128)(4,1)S(1)}, ...), branch_computations={%region_3.4_spmd, %region_4.7_spmd} | conditional | flops 4070774272 | bytes 63906876 | solution.py:100
  45.8 5.7 %select_reduce_fusion = (f32[192,10]{0,1:T(8,128)S(1)}, f32[192,10,2048]{2,0,1:T(8,128)S(1)}) fusion(pred[192,2048]{1,0:T(8,128)(4,1)S(1)} %bitcast.103, bf16[1,2048,512]{2,1,0:T(8,128)(2,1)} %get-tuple-element.118, bf16[1,192,10,256]{1,3,2,0:T(8,128)(2,1)S(1)} %get-tuple-element.209), kind=kOutput, calls=%fused_computation.4 | convolution fusion | flops 2025060480 | bytes 18161152 | tf_op jit(solution)/shard_map/while/body/eval_jaxpr/cond/branch_1_fun/rthd,rnd->rthn/dot_general | solution.py:57
  51.6 5.4 %bitcast_add_fusion = f32[1,192,10,256]{3,1,2,0:T(8,128)} fusion(f32[1,192,10,256]{3,1,2,0:T(8,128)} %get-tuple-element.120, f32[192,10,2048]{2,0,1:T(8,128)S(1)} %get-tuple-element.243, f32[192,10]{0,1:T(8,128)S(1)} %bitcast.109, pred[192,2048]{1,0:T(8,128)(4,1)S(1)} %bitcast.104, bf16[1,2048,512]{2,1,0:T(8,128)(2,1)S(1)} %copy-done.2, ...), kind=kOutput, calls=%fused_computation.9 | convolution fusion | flops 2029977600 | bytes 21135360 | tf_op jit(solution)/shard_map/while/body/eval_jaxpr/cond/branch_1_fun/rthn,rnd->rthd/dot_general | solution.py:71
  56.9 4.7 %fusion.1 = f32[192,10]{0,1:T(8,128)S(1)} fusion(f32[192,10,2048]{2,0,1:T(8,128)S(1)} %get-tuple-element.243, f32[192,10]{0,1:T(8,128)S(1)} %bitcast.110, pred[192,2048]{1,0:T(8,128)(4,1)S(1)} %bitcast.105), kind=kLoop, calls=%fused_computation.6 | loop fusion | flops 15726720 | bytes 16137216 | tf_op jit(solution)/shard_map/while/body/eval_jaxpr/cond/branch_1_fun/reduce_sum | solution.py:70
  61.6 7.6 %conditional.3 = ((f32[1,192,10]{1,2,0:T(8,128)S(1)}, f32[1,192,10,256]{3,1,2,0:T(8,128)})) conditional(s32[]{:T(128)} %convert_element_type.53, (f32[1,192,10]{1,2,0:T(8,128)S(1)}, f32[1,192,10,256]{3,1,2,0:T(8,128)}) %tuple.33, (s32[768]{0:T(1024)S(1)}, s32[192]{0:T(256)S(1)}, bf16[1,192,10,256]{1,3,2,0:T(8,128)(2,1)S(1)}, ...), branch_computations={%region_7.8_spmd, %region_8.11_spmd} | conditional | flops 1527307776 | bytes 24442648 | solution.py:100
  61.7 0.1 broadcast_compare_fusion
  61.8 1.7 select_reduce_fusion.1
  63.6 3.7 %bitcast_add_fusion.2 = f32[1,192,10,256]{3,1,2,0:T(8,128)} fusion(f32[1,192,10,256]{3,1,2,0:T(8,128)} %get-tuple-element.138, f32[192,10,768]{2,0,1:T(8,128)S(1)} %get-tuple-element.241, f32[192,10]{0,1:T(8,128)S(1)} %get-tuple-element.239, pred[192,768]{1,0:T(8,128)(4,1)S(1)} %broadcast_compare_fusion, f32[192,10]{0,1:T(8,128)S(1)} %get-tuple-element.238, ...), kind=kOutput, calls=%fused_computation.31 | convolution fusion | flops 761856000 | bytes 10403840 | tf_op jit(solution)/shard_map/while/body/eval_jaxpr/cond/branch_1_fun/rthn,rnd->rthd/dot_general | solution.py:71
  67.3 1.7 fusion.17
  69.3 2.0 divide_convert_fusion
  71.3 1.4 copy.37
  72.7 1.7 multiply_reduce_fusion
  74.5 0.3 dynamic_update_slice.3
  74.8 0.6 copy-done.4
  75.4 2.1 gather_fusion.2
  77.6 1.9 fusion.39
  79.5 2.3 copy.39
  81.8 24.0 %all-reduce.3.cloned.1.call-done = f32[8,2560]{1,0:T(8,128)} async-done(((f32[8,2560]{1,0:T(8,128)}), f32[8,2560]{1,0:T(8,128)}) %all-reduce.3.cloned.1.call-update) | async-done | bytes 81936 | tf_op jit(solution)/shard_map/psum | solution.py:140
  105.8 38.5 %psum.29 = bf16[8,2560]{1,0:T(8,128)(2,1)S(1)} all-reduce(f32[8,2560]{1,0:T(8,128)} %all-reduce.3.cloned.1.call-done), channel_id=1, replica_groups=mesh['gx'=8,'gy'=4] {'gx'}, use_global_device_ids=true, to_apply=%region_12.13 | all-reduce | flops 20480 | bytes 122880 | tf_op jit(solution)/shard_map/psum | solution.py:140
  144.3 0.9 fusion.37
  145.2 38.6 %all-gather = bf16[32,80,8]{1,2,0:T(8,128)(2,1)S(1)} all-gather(bf16[1,80,8]{1,2,0:T(8,128)(2,1)S(1)} %fusion.37), channel_id=1, replica_groups=mesh['gx'=8,'gy'=4] {'gx','gy'}, dimensions={0}, use_global_device_ids=true | all-gather | bytes 42240 | tf_op jit(solution)/shard_map/all_gather | solution.py:145
  183.8 0.1 reshape.940
  184.0 0.1 multiply_reduce_fusion.1
  184.1 17.2 %fusion.56 = (f32[8]{0:T(128)S(1)}, f32[8,8000]{1,0:T(8,128)S(1)}) fusion(bf16[8000,2560]{1,0:T(8,128)(2,1)} %param.22, f32[2560,8]{0,1:T(8,128)S(1)} %reshape.940, f32[2560]{0:T(1024)} %convert_element_type.62, f32[8]{0:T(128)S(1)} %add_rsqrt_fusion), kind=kOutput, calls=%fused_computation.123 | convolution fusion | flops 327805440 | bytes 41308224 | tf_op jit(solution)/shard_map/dot_general | solution.py:151
  201.3 36.9 %pmax.7 = f32[8]{0:T(128)S(1)} all-reduce(f32[8]{0:T(128)S(1)} %get-tuple-element.250), channel_id=1, replica_groups=mesh['gx'=8,'gy'=4] {'gx','gy'}, use_global_device_ids=true, to_apply=%region_15.16 | all-reduce | flops 8 | bytes 64 | tf_op jit(solution)/shard_map/pmax | solution.py:159
  238.2 0.3 select_reduce_fusion.2
  238.5 41.2 %all-reduce = (f32[8]{0:T(128)S(1)}, f32[8]{0:T(128)S(1)}) all-reduce(f32[8]{0:T(128)S(1)} %get-tuple-element.227, f32[8]{0:T(128)S(1)} %get-tuple-element.226), channel_id=1, replica_groups=mesh['gx'=8,'gy'=4] {'gx','gy'}, use_global_device_ids=true, to_apply=%region_17.18 | all-reduce | flops 16 | bytes 128 | tf_op jit(solution)/shard_map/psum | solution.py:160
  279.7 0.5 fusion.53
  (41 shorter events, 0.4 us)
Async XLA Ops:
  7.2 137.2 %copy-start = (bf16[2560,80]{0,1:T(8,128)(2,1)S(1)}, bf16[2560,80]{0,1:T(8,128)(2,1)}, u32[]{:S(2)}) copy-start(bf16[2560,80]{0,1:T(8,128)(2,1)} %param.19) | copy-start | bytes 1228804
  7.2 37.0 %copy-start.7 = (s32[8]{0:T(128)S(1)}, s32[8]{0:T(128)}, u32[]{:S(2)}) copy-start(s32[8]{0:T(128)} %param.23) | copy-start | bytes 100
  7.2 38.6 %all-gather.3.cloned.1.call-start = ((), (), s32[]{:S(2)}) async-start(), calls=%async_computation | async-start | bytes 2621440 | tf_op jit(solution)/shard_map/all_gather | solution.py:122
  7.9 97.9 %all-reduce.3.cloned.1.call-start = ((), (), s32[]{:S(2)}) async-start(), calls=%async_computation.1 | async-start | bytes 163840 | tf_op jit(solution)/shard_map/psum | solution.py:140
  45.8 5.7 %copy-start.2 = (bf16[1,2048,512]{2,1,0:T(8,128)(2,1)S(1)}, bf16[1,2048,512]{2,1,0:T(8,128)(2,1)}, u32[]{:S(2)}) copy-start(bf16[1,2048,512]{2,1,0:T(8,128)(2,1)} %get-tuple-element.118) | copy-start | bytes 6291460 | tf_op jit(solution)/shard_map/while/body/eval_jaxpr/cond
  69.2 6.2 %copy-start.1 = (bf16[1,2048,512]{2,1,0:T(8,128)(2,1)S(1)}, bf16[1,2048,512]{2,1,0:T(8,128)(2,1)}, u32[]{:S(2)}) copy-start(bf16[1,2048,512]{2,1,0:T(8,128)(2,1)} %all-gather.3.cloned.1.call-done) | copy-start | bytes 6291460
  72.7 4.8 %copy-start.3 = (bf16[512,512]{1,0:T(8,128)(2,1)S(1)}, bf16[512,512]{1,0:T(8,128)(2,1)}, u32[]{:S(2)}) copy-start(bf16[512,512]{1,0:T(8,128)(2,1)} %gather_fusion.1) | copy-start | bytes 1572868
  74.8 0.6 copy-start.4
  184.1 54.1 %copy-start.6 = (s32[8]{0:T(128)S(1)}, s32[8]{0:T(128)}, u32[]{:S(2)}) copy-start(s32[8]{0:T(128)} %broadcast_subtract_fusion) | copy-start | bytes 100
  238.2 42.0 %copy-start.5 = (f32[8]{0:T(128)}, f32[8]{0:T(128)S(1)}, u32[]{:S(2)}) copy-start(f32[8]{0:T(128)S(1)} %pmax.7) | copy-start | bytes 100
Sparse Core Ops, SparseCore 0:
  9.6 29.4 all-gather.2
  75.5 30.2 all-reduce.2
